TPU v7x, 32 devices: a whole 2x2x4 slice. The times are simulated.
32 devices in a mesh: ctx: 4 (over y, x), dp: 4 (over z), tp: 2 (over core).
Axes of the slice: x: 2, y: 2, z: 4, core: 2. Of those that a mesh axis runs over, the one named last changes fastest.
Arguments:
- queries: bfloat16 [4, 512, 32, 128], P('dp', 'ctx', 'tp'), may hold values from -21 to 21
- keys: bfloat16 [4, 512, 4, 128], P('dp', 'ctx', 'tp'), may hold values from -6 to 6
- values: bfloat16 [4, 512, 4, 128], P('dp', 'ctx', 'tp'), may hold values from -6 to 6
- output_cotangent: bfloat16 [4, 512, 32, 128], P('dp', 'ctx', 'tp'), may hold values from -6 to 6
- features: bfloat16 [4, 512, 4096], P('dp', 'ctx'), may hold values from -60 to 60
- doc_lengths: int32 [4, 48], P('dp'), may hold values from 1 to 16, 512 in all within a row
- rope_num: int32 [64], replicated, may hold values from 1 to 40
- rope_den: int32 [64], replicated, may hold values from 1 to 8
- param: float32 [4096, 512], P('dp', 'tp'), may hold values from -0.4375 to 0.4375
- first_moment_state: float32 [4096, 512], P('dp', 'tp'), may hold values from -4 to 4
- second_moment_state: float32 [4096, 512], P('dp', 'tp'), may hold values from 0.05 to 1
Outputs:
- grad_queries: bfloat16 [4, 512, 32, 128], P('dp', 'ctx', 'tp')
- grad_keys: bfloat16 [4, 512, 4, 128], P('dp', 'ctx', 'tp')
- value_gradient: bfloat16 [4, 512, 4, 128], P('dp', 'ctx', 'tp')
- new_param: float32 [4096, 512], P('dp', 'tp')
- new_first: float32 [4096, 512], P('dp', 'tp')
- new_second: float32 [4096, 512], P('dp', 'tp')
Inputs may be any that keep to these rules, and one draw needn't show every extreme that they name: `doc_lengths`: each row's 48 lengths sum to 512, and the largest of each row is exactly 16.
All inputs are finite; a program needn't handle non-finite values.
Results may differ from a plain program's by a relative error of at most 0.0064.
Values may be sent and summed in bfloat16 or wider, within the bound.
No kernel may reach another device: no remote copies, remote signals or barrier semaphores. Data moves between devices by JAX's collectives and lax.ppermute only.
A program may use at most 64 MiB of HBM per device.

v0:
```python
from functools import reduce
import math
import jax
import jax.numpy as jnp
from jax import lax
from jax.sharding import PartitionSpec as P

ROPE_BASE = 500000.0
NEG_FILL = -1e30
CLIP_NORM = 1000.0
LEARN_RATE = 0.0001
DECAY_RATE = 0.1
BETA_ONE = 0.9
BETA_TWO = 0.95
ADAM_EPS = 1e-08
FIRST_FIX = 1.0 - 0.9**10
SECOND_FIX = 1.0 - 0.95**10


def shifted(array, axis, by):
    peers = lax.axis_size(axis)
    pairs = [(i, i + by) for i in range(peers) if 0 <= i + by < peers]
    return lax.ppermute(array, axis, pairs)


def doc_layout(lengths_row, token_index):
    doc_ends = jnp.cumsum(lengths_row)
    passed = doc_ends[None, :] <= token_index[:, None]
    doc_start = jnp.max(jnp.where(passed, doc_ends[None, :], 0), axis=1)
    doc_id = jnp.sum(passed.astype(jnp.int32), axis=1)
    return (doc_id, (token_index - doc_start).astype(jnp.float32))


def rope_tables(position, rope_num, rope_den, head_dim):
    expo = jnp.arange(head_dim // 2, dtype=jnp.float32) * (2.0 / head_dim)
    freq = (
        jnp.exp(-math.log(ROPE_BASE) * expo)
        * rope_den.astype(jnp.float32)
        / rope_num.astype(jnp.float32)
    )
    angle = position[:, None] * freq[None, :]
    cosine = jnp.concatenate([jnp.cos(angle), jnp.cos(angle)], axis=1)
    sine = jnp.concatenate([jnp.sin(angle), jnp.sin(angle)], axis=1)
    return (cosine[:, None, :], sine[:, None, :])


def rotate(vectors, cosine, sine):
    half = vectors.shape[-1] // 2
    turned = jnp.concatenate([-vectors[..., half:], vectors[..., :half]], axis=-1)
    return vectors * cosine + turned * sine


def unrotate(grads_in, cosine, sine):
    half = grads_in.shape[-1] // 2
    scaled = grads_in * sine
    turned = jnp.concatenate([scaled[..., half:], -scaled[..., :half]], axis=-1)
    return grads_in * cosine + turned


def adam_update(param, first_moment_state, second_moment_state, weight_gradient, grad_total):
    clip_factor = jnp.minimum(jnp.float32(1.0), CLIP_NORM / jnp.sqrt(grad_total))
    clipped = weight_gradient * clip_factor
    new_first = BETA_ONE * first_moment_state + (1.0 - BETA_ONE) * clipped
    new_second = BETA_TWO * second_moment_state + (1.0 - BETA_TWO) * clipped * clipped
    step_size = new_first / FIRST_FIX / (jnp.sqrt(new_second / SECOND_FIX) + ADAM_EPS)
    new_param = param - LEARN_RATE * (step_size + DECAY_RATE * param)
    return (new_param, new_first, new_second)


def local(
    queries,
    keys,
    values,
    output_cotangent,
    features,
    doc_lengths,
    rope_num,
    rope_den,
    param,
    first_moment_state,
    second_moment_state,
):
    tok_rows = queries.shape[1]
    head_count = queries.shape[2]
    head_dim = queries.shape[3]
    kv_count = keys.shape[2]
    group_size = head_count // kv_count
    n_ctx = lax.axis_size("ctx")
    place = lax.axis_index("ctx")
    seq_len = tok_rows * n_ctx
    doc_most = seq_len // 32
    reach = (doc_most + tok_rows - 2) // tok_rows
    scale = head_dim ** (-0.5)
    lengths_row = doc_lengths[0]
    own_index = place * tok_rows + jnp.arange(tok_rows, dtype=jnp.int32)
    own_doc, position = doc_layout(lengths_row, own_index)
    cosine, sine = rope_tables(position, rope_num, rope_den, head_dim)
    rotated_query_rows = rotate(queries[0].astype(jnp.float32), cosine, sine).astype(jnp.bfloat16)
    rotated_query_rows = rotated_query_rows.reshape(tok_rows, kv_count, group_size, head_dim)
    rotated_key_rows = rotate(keys[0].astype(jnp.float32), cosine, sine).astype(jnp.bfloat16)
    grad_out = output_cotangent[0].reshape(tok_rows, kv_count, group_size, head_dim)
    kv_pair = jnp.stack([rotated_key_rows, values[0]])
    pairs = [kv_pair]
    offset = 1
    kv_pair = shifted(kv_pair, "ctx", 1)
    pairs.append(kv_pair)
    masks = []
    for offset in range(reach + 1):
        key_index = (place - offset) * tok_rows + jnp.arange(tok_rows, dtype=jnp.int32)
        key_doc = doc_layout(lengths_row, key_index)[0]
        valid = (
            (key_index[None, :] >= 0)
            & (key_index[None, :] <= own_index[:, None])
            & (key_doc[None, :] == own_doc[:, None])
        )
        masks.append(valid)
    score_list = []
    for pair_in, valid_in in zip(pairs, masks):
        raw = (
            jnp.einsum(
                "qhgd,khd->hgqk", rotated_query_rows, pair_in[0], preferred_element_type=jnp.float32
            )
            * scale
        )
        score_list.append(jnp.where(valid_in, raw, NEG_FILL))
    row_top = reduce(
        jnp.maximum, [jnp.max(scores, axis=-1, keepdims=True) for scores in score_list]
    )
    weight_list = [
        jnp.where(valid_in, jnp.exp(scores - row_top), 0.0)
        for scores, valid_in in zip(score_list, masks)
    ]
    row_total = reduce(
        jnp.add, [jnp.sum(weights, axis=-1, keepdims=True) for weights in weight_list]
    )
    prob_list = [weights / row_total for weights in weight_list]
    low_list = [probs.astype(jnp.bfloat16) for probs in prob_list]
    attn_out = reduce(
        jnp.add,
        [
            jnp.einsum("hgqk,khd->qhgd", probs_low, pair_in[1], preferred_element_type=jnp.float32)
            for probs_low, pair_in in zip(low_list, pairs)
        ],
    )
    delta = jnp.einsum("qhgd,qhgd->hgq", grad_out.astype(jnp.float32), attn_out)[..., None]
    query_terms = []
    key_terms = []
    for pair_in, probs, probs_low, valid_in in zip(pairs, prob_list, low_list, masks):
        dprobs = jnp.einsum(
            "qhgd,khd->hgqk", grad_out, pair_in[1], preferred_element_type=jnp.float32
        )
        dscores = (probs * (dprobs - delta)).astype(jnp.bfloat16)
        q_part = (
            jnp.einsum("hgqk,khd->qhgd", dscores, pair_in[0], preferred_element_type=jnp.float32)
            * scale
        )
        k_part = (
            jnp.einsum(
                "hgqk,qhgd->khd", dscores, rotated_query_rows, preferred_element_type=jnp.float32
            )
            * scale
        )
        v_part = jnp.einsum(
            "hgqk,qhgd->khd", probs_low, grad_out, preferred_element_type=jnp.float32
        )
        q_part, kv_part = (q_part, jnp.stack([k_part, v_part]))
        query_terms.append(q_part)
        key_terms.append(kv_part)
    query_grad = reduce(jnp.add, query_terms)
    key_total = key_terms[reach]
    offset = 0
    key_total = (
        shifted(key_total.astype(jnp.bfloat16), "ctx", -1).astype(key_total.dtype)
        + key_terms[offset]
    )
    grad_q = unrotate(query_grad.reshape(tok_rows, head_count, head_dim), cosine, sine).astype(
        jnp.bfloat16
    )
    grad_k = unrotate(key_total[0], cosine, sine).astype(jnp.bfloat16)
    grad_v = key_total[1].astype(jnp.bfloat16)
    feats = features[0]
    width = feats.shape[1]
    value_flat = grad_v.reshape(tok_rows, kv_count * head_dim)
    own_rows = param.shape[0]
    n_dp = lax.axis_size("dp")
    piece_rows = own_rows // n_ctx
    permuted = (
        feats.reshape(tok_rows, n_dp, n_ctx, piece_rows)
        .transpose(0, 2, 1, 3)
        .reshape(tok_rows, width)
    )
    pieces = lax.psum_scatter(
        lax.dot_general(
            permuted, value_flat, (((0,), (0,)), ((), ())), preferred_element_type=jnp.float32
        ),
        ("ctx", "dp"),
        scatter_dimension=0,
        tiled=True,
    )
    weight_gradient = lax.all_gather(pieces, "ctx", axis=0, tiled=True)
    norm_part = jnp.sum(weight_gradient * weight_gradient)
    grad_total = lax.psum(norm_part, ("dp", "tp"))
    new_param, new_first, new_second = adam_update(
        param, first_moment_state, second_moment_state, weight_gradient, grad_total
    )
    return (grad_q[None], grad_k[None], grad_v[None], new_param, new_first, new_second)


def solution(mesh):
    placed = (
        P("dp", "ctx", "tp", None),
        P("dp", "ctx", "tp", None),
        P("dp", "ctx", "tp", None),
        P("dp", "ctx", "tp", None),
        P("dp", "ctx", None),
        P("dp", None),
        P(),
        P(),
        P("dp", "tp"),
        P("dp", "tp"),
        P("dp", "tp"),
    )
    return jax.shard_map(
        local,
        mesh=mesh,
        in_specs=placed,
        out_specs=(
            P("dp", "ctx", "tp", None),
            P("dp", "ctx", "tp", None),
            P("dp", "ctx", "tp", None),
            P("dp", "tp"),
            P("dp", "tp"),
            P("dp", "tp"),
        ),
        check_vma=False,
    )
```

profile of v0, /device:TPU:0, one launch (start us, length us, event | category | flops | bytes accessed | tf_op | source)
XLA Modules:
  0.0 216.5 jit_solution(16039566260402643105)
XLA Ops:
  13.5 5.5 %collective-permute-start = (bf16[2,128,2,128]{3,1,2,0:T(8,128)(2,1)}, bf16[2,128,2,128]{3,1,2,0:T(8,128)(2,1)}, u32[]{:S(2)}, u32[]{:S(2)}) collective-permute-start(bf16[2,128,2,128]{3,1,2,0:T(8,128)(2,1)} %pad_maximum_fusion), channel_id=1, source_target_pairs={{0,8},{8,16},{16,24},{1,9},{9,17},{17,25},{2,10},{10,18},{18,26},{... | collective-permute-start | bytes 393224 | tf_op jit(solution)/shard_map/ppermute | solution.py:23
  21.6 1.3 fusion.22
  22.9 2.4 %copy.138 = f32[128,2,8,64]{0,3,2,1:T(8,128)} copy(f32[128,2,8,64]{3,2,1,0:T(8,128)} %get-tuple-element.40) | data formatting | bytes 1048576 | tf_op jit(solution)/shard_map/concatenate | solution.py:49
  25.3 1.2 copy.139
  28.8 1.4 fusion.24
  30.5 1.2 copy.164
  31.8 1.6 copy.168
  38.5 1.2 fusion.3
  40.5 1.4 fusion.12
  42.0 1.6 fusion.11
  43.9 1.3 collective-permute-start.1
  45.6 5.2 %collective-permute-done.1 = bf16[2,128,2,128]{3,1,2,0:T(8,128)(2,1)S(1)} collective-permute-done((bf16[2,128,2,128]{3,1,2,0:T(8,128)(2,1)S(1)}, bf16[2,128,2,128]{3,1,2,0:T(8,128)(2,1)S(1)}, u32[]{:S(2)}, u32[]{:S(2)}) %collective-permute-start.1) | collective-permute-done | bytes 131104 | tf_op jit(solution)/shard_map/ppermute | solution.py:23
  51.5 2.6 %convolution_bitcast_fusion = f32[4096,256]{0,1:T(8,128)} fusion(bf16[128,256]{0,1:T(8,128)(2,1)S(1)} %bitcast.172, bf16[128,4096]{0,1:T(8,128)(2,1)S(1)} %bitcast.170), kind=kOutput, calls=%fused_computation | convolution fusion | flops 268435456 | bytes 5308416 | tf_op jit(solution)/shard_map/dot_general | solution.py:193
  55.4 1.3 copy.166
  56.7 1.3 copy.170
  58.0 2.5 %copy.172 = f32[1024,256]{0,1:T(8,128)} copy(f32[1024,256]{1,0:T(8,128)} %param.19) | data formatting | bytes 2097152 | tf_op args[8]
  61.7 90.6 %reduce-scatter.2.cloned.1.call-done = f32[256,256]{0,1:T(8,128)} async-done(((f32[4096,256]{0,1:T(8,128)}), f32[256,256]{0,1:T(8,128)}) %reduce-scatter.2.cloned.1.call-update) | async-done | bytes 262160 | tf_op jit(solution)/shard_map/reduce_scatter | solution.py:192
  157.1 22.0 %all-gather.2.cloned.1.call-done = f32[1024,256]{0,1:T(8,128)} async-done(((f32[256,256]{0,1:T(8,128)}), f32[1024,256]{0,1:T(8,128)}) %all-gather.2.cloned.1.call-update) | async-done | bytes 1048592 | tf_op jit(solution)/shard_map/all_gather | solution.py:200
  179.1 2.2 %multiply_reduce_fusion.1 = f32[]{:T(128)} fusion(f32[1024,256]{0,1:T(8,128)} %all-gather.2.cloned.1.call-done), kind=kLoop, calls=%fused_computation.50 | loop fusion | flops 524287 | bytes 1048580 | tf_op jit(solution)/shard_map/reduce_sum | solution.py:201
  182.0 16.9 %psum.7 = f32[]{:T(128)} all-reduce(f32[]{:T(128)} %multiply_reduce_fusion.1), channel_id=1, replica_groups=mesh['ctx'=4,'dp'=4,'tp'=2] {'dp','tp'}, use_global_device_ids=true, to_apply=%region_10.11 | all-reduce | flops 1 | bytes 8 | tf_op jit(solution)/shard_map/psum | solution.py:202
  199.7 3.7 %multiply_subtract_fusion = (f32[1024,256]{0,1:T(8,128)}, f32[1024,256]{0,1:T(8,128)}, f32[1024,256]{0,1:T(8,128)S(1)}) fusion(f32[1024,256]{0,1:T(8,128)} %copy.172, f32[1024,256]{0,1:T(8,128)} %all-gather.2.cloned.1.call-done, f32[]{:T(128)S(6)} %min_shard_map.3, f32[1024,256]{0,1:T(8,128)S(1)} %copy-done.1, f32[1024,256]{0,1:T(8,128)S(1)} %copy-done.2), kind=kLoop, calls=%fused_computation.48 | loop fusion | flops 4194304 | bytes 7340036 | tf_op jit(solution)/shard_map/sub | solution.py:66
  203.3 2.5 %copy.175 = f32[1024,256]{1,0:T(8,128)} copy(f32[1024,256]{0,1:T(8,128)} %get-tuple-element.35) | data formatting | bytes 2097152
  205.9 2.5 %copy.176 = f32[1024,256]{1,0:T(8,128)} copy(f32[1024,256]{0,1:T(8,128)} %get-tuple-element.36) | data formatting | bytes 2097152
  208.4 1.3 copy.177
  (88 shorter events, 26.4 us)
Async XLA Ops:
  7.2 145.1 %reduce-scatter.2.cloned.1.call-start = ((), (), s32[]{:S(2)}) async-start(), calls=%async_computation.1 | async-start | bytes 4456448 | tf_op jit(solution)/shard_map/reduce_scatter | solution.py:192
  13.5 21.0 %collective-permute-start = (bf16[2,128,2,128]{3,1,2,0:T(8,128)(2,1)}, bf16[2,128,2,128]{3,1,2,0:T(8,128)(2,1)}, u32[]{:S(2)}, u32[]{:S(2)}) collective-permute-start(bf16[2,128,2,128]{3,1,2,0:T(8,128)(2,1)} %pad_maximum_fusion), channel_id=1, source_target_pairs={{0,8},{8,16},{16,24},{1,9},{9,17},{17,25},{2,10},{10,18},{18,26},{... | collective-permute-start | bytes 393224 | tf_op jit(solution)/shard_map/ppermute | solution.py:23
  21.6 5.4 %copy-start.11 = (bf16[1,128,2,128]{3,2,1,0:T(2,128)(2,1)S(1)}, bf16[1,128,2,128]{3,2,1,0:T(2,128)(2,1)}, u32[]{:S(2)}) copy-start(bf16[1,128,2,128]{3,2,1,0:T(2,128)(2,1)} %param.12) | copy-start | bytes 196612
  25.3 5.2 %copy-start.3 = (bf16[1,128,16,128]{3,2,1,0:T(8,128)(2,1)S(1)}, bf16[1,128,16,128]{3,2,1,0:T(8,128)(2,1)}, u32[]{:S(2)}) copy-start(bf16[1,128,16,128]{3,2,1,0:T(8,128)(2,1)} %param.14) | copy-start | bytes 1572868
  28.0 2.5 %copy-start.10 = (bf16[128,2,128,1]{2,0,3,1:T(8,128)(2,1)}, bf16[128,2,128,1]{2,0,3,1:T(8,128)(2,1)S(1)}, u32[]{:S(2)}) copy-start(bf16[128,2,128,1]{2,0,3,1:T(8,128)(2,1)S(1)} %fusion.40) | copy-start | bytes 196612
  33.4 2.6 %copy-start.12 = (bf16[128,2,8,128]{0,3,2,1:T(8,128)(2,1)S(1)}, bf16[128,2,8,128]{0,3,2,1:T(8,128)(2,1)}, u32[]{:S(2)}) copy-start(bf16[128,2,8,128]{0,3,2,1:T(8,128)(2,1)} %copy.164) | copy-start | bytes 1572868
  36.0 2.0 copy-start.14
  42.0 1.9 copy-start.15
  42.0 8.8 %copy-start.13 = (f32[1,128,2,128]{3,1,2,0:T(8,128)S(1)}, f32[1,128,2,128]{3,1,2,0:T(8,128)}, u32[]{:S(2)}) copy-start(f32[1,128,2,128]{3,1,2,0:T(8,128)} %convolution_bitcast_fusion.5) | copy-start | bytes 393220
  42.0 9.5 %copy-start = (bf16[128,4,4,256]{0,3,2,1:T(8,128)(2,1)S(1)}, bf16[128,4,4,256]{0,3,2,1:T(8,128)(2,1)}, u32[]{:S(2)}) copy-start(bf16[128,4,4,256]{0,3,2,1:T(8,128)(2,1)} %copy.169) | copy-start | bytes 3145732
  43.6 2.0 copy-start.4
  43.9 6.9 %collective-permute-start.1 = (bf16[2,128,2,128]{3,1,2,0:T(8,128)(2,1)S(1)}, bf16[2,128,2,128]{3,1,2,0:T(8,128)(2,1)S(1)}, u32[]{:S(2)}, u32[]{:S(2)}) collective-permute-start(bf16[2,128,2,128]{3,1,2,0:T(8,128)(2,1)S(1)} %pad_maximum_fusion.1), channel_id=1, source_target_pairs={{8,0},{16,8},{24,16},{9,1},{17,9},{25,17},{10,2},{18,10},{26,18},{... | collective-permute-start | bytes 393224 | tf_op jit(solution)/shard_map/ppermute | solution.py:23
  50.9 0.6 copy-start.8
  54.1 1.2 copy-start.6
  54.1 2.5 %copy-start.7 = (f32[1024,256]{1,0:T(8,128)S(1)}, f32[1024,256]{1,0:T(8,128)}, u32[]{:S(2)}) copy-start(f32[1024,256]{1,0:T(8,128)} %param.21) | copy-start | bytes 3145732
  54.2 98.2 %copy-start.5 = (bf16[2,8,128,128]{2,3,1,0:T(8,128)(2,1)S(1)}, bf16[2,8,128,128]{2,3,1,0:T(8,128)(2,1)}, u32[]{:S(2)}) copy-start(bf16[2,8,128,128]{2,3,1,0:T(8,128)(2,1)} %copy-done.4) | copy-start | bytes 1572868
  54.2 125.0 %all-gather.2.cloned.1.call-start = ((), (), s32[]{:S(2)}) async-start(), calls=%async_computation.2 | async-start | bytes 1310720 | tf_op jit(solution)/shard_map/all_gather | solution.py:200
  154.7 1.6 copy-start.9
  155.0 44.6 %copy-start.1 = (f32[1024,256]{0,1:T(8,128)S(1)}, f32[1024,256]{0,1:T(8,128)}, u32[]{:S(2)}) copy-start(f32[1024,256]{0,1:T(8,128)} %copy.166) | copy-start | bytes 3145732
  155.0 44.6 %copy-start.2 = (f32[1024,256]{0,1:T(8,128)S(1)}, f32[1024,256]{0,1:T(8,128)}, u32[]{:S(2)}) copy-start(f32[1024,256]{0,1:T(8,128)} %copy.170) | copy-start | bytes 3145732
Sparse Core Ops, SparseCore 0:
  54.3 97.9 reduce-scatter.1
  154.1 24.9 all-gather.1
where the time goes:
time: 218 us; the launch traced here: 217 us
  waiting for transfers between devices  118 us (54%)
  local copies, waits for them, and re-layouts  26 us (12%)
  other arithmetic  19.8 us (9%)
  blocking collectives  16.9 us (8%)
  between operations  15.2 us (7%)
  matrix products  13.7 us (6%)
  starting transfers between devices  7.07 us (3%)
    reduce_scatter x1, waiting for transfers between devices, local(): lax.psum_scatter(lax.dot_general(permuted, value_flat, (((0,), (0,)), (()...  90.6 us
    all_gather x1, waiting for transfers between devices, local(): weight_gradient = lax.all_gather(pieces, 'ctx', axis=0, tiled=True)  22 us
    unnamed x42, local copies, waits for them, and re-layouts  16.9 us
    psum x1, blocking collectives, local(): grad_total = lax.psum(norm_part, ('dp', 'tp'))  16.9 us
    ppermute x2, starting transfers between devices, shifted(): return lax.ppermute(array, axis, pairs)  6.81 us
    ppermute x2, waiting for transfers between devices, shifted(): return lax.ppermute(array, axis, pairs)  5.25 us
  transfers between devices with their start and end apart: 4, of which 3 were waited for; matrix products, arithmetic and copies ran while one was open for 12% of the time, Pallas kernels for 0%

commit v1 on v0

--- a/solution.py
+++ b/solution.py
@@ -15,6 +15,18 @@
 ADAM_EPS = 1e-08
 FIRST_FIX = 1.0 - 0.9**10
 SECOND_FIX = 1.0 - 0.95**10
+
+
+def doubled_up(x, axis, dim):
+    ways, here = (lax.axis_size(axis), lax.axis_index(axis))
+    grown, reach = (x, 1)
+    while reach < ways:
+        theirs = lax.ppermute(grown, axis, [(d, d ^ reach) for d in range(ways)])
+        mine_first = jnp.concatenate([grown, theirs], axis=dim)
+        theirs_first = jnp.concatenate([theirs, grown], axis=dim)
+        grown = jnp.where(here & reach == 0, mine_first, theirs_first)
+        reach = 2 * reach
+    return grown
 
 
 def shifted(array, axis, by):
@@ -197,7 +209,7 @@
         scatter_dimension=0,
         tiled=True,
     )
-    weight_gradient = lax.all_gather(pieces, "ctx", axis=0, tiled=True)
+    weight_gradient = doubled_up(pieces, "ctx", 0)
     norm_part = jnp.sum(weight_gradient * weight_gradient)
     grad_total = lax.psum(norm_part, ("dp", "tp"))
     new_param, new_first, new_second = adam_update(

time: 218 us -> 204 us (0.936)
  waiting for transfers between devices: 118 us -> 108 us
  blocking collectives: 16.9 us -> 14.2 us
    all_gather x1 -> x0, waiting for transfers between devices: 22 us -> none  [local(): weight_gradient = lax.all_gather(pieces, 'ctx', axis=0, tiled=True)]
    ppermute x0 -> x2, waiting for transfers between devices: none -> 13.8 us  [doubled_up(): theirs = lax.ppermute(grown, axis, [(d, d ^ reach) for d in range(ways)])]
    psum x1, blocking collectives: 16.9 us -> 14.2 us  [local(): grad_total = lax.psum(norm_part, ('dp', 'tp'))]
    unnamed x42 -> x46, local copies, waits for them, and re-layouts: 16.9 us -> 17.2 us
  transfers between devices with their start and end apart: 4 -> 5, of which waited for: 3 -> 4; matrix products, arithmetic and copies ran while one was open for 12% -> 13% of each run, Pallas kernels for 0% -> 0%
where the time goes in v1:
time: 204 us; the launch traced here: 203 us
  waiting for transfers between devices  108 us (53%)
  local copies, waits for them, and re-layouts  26.3 us (13%)
  other arithmetic  19.5 us (10%)
  between operations  15.1 us (7%)
  blocking collectives  14.2 us (7%)
  matrix products  12.9 us (6%)
  starting transfers between devices  7.67 us (4%)
    reduce_scatter x1, waiting for transfers between devices, local(): lax.psum_scatter(lax.dot_general(permuted, value_flat, (((0,), (0,)), (()...  88.8 us
    unnamed x46, local copies, waits for them, and re-layouts  17.2 us
    psum x1, blocking collectives, local(): grad_total = lax.psum(norm_part, ('dp', 'tp'))  14.2 us
    ppermute x2, waiting for transfers between devices, doubled_up(): theirs = lax.ppermute(grown, axis, [(d, d ^ reach) for d in range(ways)])  13.8 us
    ppermute x2, starting transfers between devices, shifted(): return lax.ppermute(array, axis, pairs)  7 us
    ppermute x2, waiting for transfers between devices, shifted(): return lax.ppermute(array, axis, pairs)  5.07 us
  transfers between devices with their start and end apart: 5, of which 4 were waited for; matrix products, arithmetic and copies ran while one was open for 13% of the time, Pallas kernels for 0%

profile of v1, /device:TPU:0, one launch (start us, length us, event | category | flops | bytes accessed | tf_op | source)
XLA Modules:
  0.0 203.3 jit_solution(2732987464669566805)
XLA Ops:
  13.5 5.5 %collective-permute-start = (bf16[2,128,2,128]{3,1,2,0:T(8,128)(2,1)}, bf16[2,128,2,128]{3,1,2,0:T(8,128)(2,1)}, u32[]{:S(2)}, u32[]{:S(2)}) collective-permute-start(bf16[2,128,2,128]{3,1,2,0:T(8,128)(2,1)} %pad_maximum_fusion), channel_id=1, source_target_pairs={{0,8},{8,16},{16,24},{1,9},{9,17},{17,25},{2,10},{10,18},{18,26},{... | collective-permute-start | bytes 393224 | tf_op jit(solution)/shard_map/ppermute | solution.py:35
  21.6 1.3 fusion.22
  22.9 2.4 %copy.138 = f32[128,2,8,64]{0,3,2,1:T(8,128)} copy(f32[128,2,8,64]{3,2,1,0:T(8,128)} %get-tuple-element.40) | data formatting | bytes 1048576 | tf_op jit(solution)/shard_map/concatenate | solution.py:61
  25.3 1.2 copy.139
  28.9 1.4 fusion.24
  30.6 1.2 copy.164
  31.8 1.6 copy.168
  38.5 1.2 fusion.3
  40.6 1.4 fusion.12
  42.0 1.6 fusion.11
  44.0 1.5 collective-permute-start.1
  45.8 5.1 %collective-permute-done.1 = bf16[2,128,2,128]{3,1,2,0:T(8,128)(2,1)S(1)} collective-permute-done((bf16[2,128,2,128]{3,1,2,0:T(8,128)(2,1)S(1)}, bf16[2,128,2,128]{3,1,2,0:T(8,128)(2,1)S(1)}, u32[]{:S(2)}, u32[]{:S(2)}) %collective-permute-start.1) | collective-permute-done | bytes 131104 | tf_op jit(solution)/shard_map/ppermute | solution.py:35
  51.5 2.6 %convolution_bitcast_fusion = f32[4096,256]{0,1:T(8,128)} fusion(bf16[128,256]{0,1:T(8,128)(2,1)S(1)} %bitcast.172, bf16[128,4096]{0,1:T(8,128)(2,1)S(1)} %bitcast.170), kind=kOutput, calls=%fused_computation | convolution fusion | flops 268435456 | bytes 5308416 | tf_op jit(solution)/shard_map/dot_general | solution.py:205
  55.4 1.3 copy.166
  56.7 1.3 copy.170
  58.0 2.5 %copy.172 = f32[1024,256]{0,1:T(8,128)} copy(f32[1024,256]{1,0:T(8,128)} %param.19) | data formatting | bytes 2097152 | tf_op args[8]
  63.6 88.8 %reduce-scatter.2.cloned.1.call-done = f32[256,256]{0,1:T(8,128)} async-done(((f32[4096,256]{0,1:T(8,128)}), f32[256,256]{0,1:T(8,128)}) %reduce-scatter.2.cloned.1.call-update) | async-done | bytes 262160 | tf_op jit(solution)/shard_map/reduce_scatter | solution.py:204
  153.6 5.4 %collective-permute-done.2 = f32[256,256]{0,1:T(8,128)S(1)} collective-permute-done((f32[256,256]{0,1:T(8,128)}, f32[256,256]{0,1:T(8,128)S(1)}, u32[]{:S(2)}, u32[]{:S(2)}) %collective-permute-start.2) | collective-permute-done | bytes 262176 | tf_op jit(solution)/shard_map/ppermute | solution.py:24
  161.7 8.3 %collective-permute-done.3 = f32[512,256]{0,1:T(8,128)S(1)} collective-permute-done((f32[512,256]{0,1:T(8,128)S(1)}, f32[512,256]{0,1:T(8,128)S(1)}, u32[]{:S(2)}, u32[]{:S(2)}) %collective-permute-start.3) | collective-permute-done | bytes 524320 | tf_op jit(solution)/shard_map/ppermute | solution.py:24
  171.6 14.2 %psum.7 = f32[]{:T(128)} all-reduce(f32[]{:T(128)} %multiply_reduce_fusion.1), channel_id=1, replica_groups=mesh['ctx'=4,'dp'=4,'tp'=2] {'dp','tp'}, use_global_device_ids=true, to_apply=%region_10.11 | all-reduce | flops 1 | bytes 8 | tf_op jit(solution)/shard_map/psum | solution.py:214
  186.4 3.6 %multiply_subtract_fusion = (f32[1024,256]{0,1:T(8,128)}, f32[1024,256]{0,1:T(8,128)}, f32[1024,256]{0,1:T(8,128)}) fusion(f32[1024,256]{0,1:T(8,128)} %copy.172, f32[]{:T(128)S(6)} %min_shard_map.3, f32[512,256]{0,1:T(8,128)S(1)} %maximum_select_fusion.1, f32[512,256]{0,1:T(8,128)S(1)} %collective-permute-done.3, pred[]{:T(512)S(6)} %eq.35, ...), kind=kLoop, calls=%fused_computation.49 | loop fusion | flops 4980736 | bytes 7340037 | tf_op jit(solution)/shard_map/sub | solution.py:78
  190.0 2.6 %copy.175 = f32[1024,256]{1,0:T(8,128)} copy(f32[1024,256]{0,1:T(8,128)} %get-tuple-element.35) | data formatting | bytes 2097152
  192.6 2.5 %copy.176 = f32[1024,256]{1,0:T(8,128)} copy(f32[1024,256]{0,1:T(8,128)} %get-tuple-element.36) | data formatting | bytes 2097152
  195.1 1.3 copy.177
  (94 shorter events, 28.1 us)
Async XLA Ops:
  7.2 145.3 %reduce-scatter.2.cloned.1.call-start = ((), (), s32[]{:S(2)}) async-start(), calls=%async_computation.1 | async-start | bytes 4456448 | tf_op jit(solution)/shard_map/reduce_scatter | solution.py:204
  13.5 21.0 %collective-permute-start = (bf16[2,128,2,128]{3,1,2,0:T(8,128)(2,1)}, bf16[2,128,2,128]{3,1,2,0:T(8,128)(2,1)}, u32[]{:S(2)}, u32[]{:S(2)}) collective-permute-start(bf16[2,128,2,128]{3,1,2,0:T(8,128)(2,1)} %pad_maximum_fusion), channel_id=1, source_target_pairs={{0,8},{8,16},{16,24},{1,9},{9,17},{17,25},{2,10},{10,18},{18,26},{... | collective-permute-start | bytes 393224 | tf_op jit(solution)/shard_map/ppermute | solution.py:35
  21.6 5.4 %copy-start.13 = (bf16[1,128,2,128]{3,2,1,0:T(2,128)(2,1)S(1)}, bf16[1,128,2,128]{3,2,1,0:T(2,128)(2,1)}, u32[]{:S(2)}) copy-start(bf16[1,128,2,128]{3,2,1,0:T(2,128)(2,1)} %param.12) | copy-start | bytes 196612
  25.3 5.2 %copy-start.4 = (bf16[1,128,16,128]{3,2,1,0:T(8,128)(2,1)S(1)}, bf16[1,128,16,128]{3,2,1,0:T(8,128)(2,1)}, u32[]{:S(2)}) copy-start(bf16[1,128,16,128]{3,2,1,0:T(8,128)(2,1)} %param.14) | copy-start | bytes 1572868
  28.0 2.5 %copy-start.11 = (bf16[128,2,128,1]{2,0,3,1:T(8,128)(2,1)}, bf16[128,2,128,1]{2,0,3,1:T(8,128)(2,1)S(1)}, u32[]{:S(2)}) copy-start(bf16[128,2,128,1]{2,0,3,1:T(8,128)(2,1)S(1)} %fusion.40) | copy-start | bytes 196612
  33.4 2.6 %copy-start.14 = (bf16[128,2,8,128]{0,3,2,1:T(8,128)(2,1)S(1)}, bf16[128,2,8,128]{0,3,2,1:T(8,128)(2,1)}, u32[]{:S(2)}) copy-start(bf16[128,2,8,128]{0,3,2,1:T(8,128)(2,1)} %copy.164) | copy-start | bytes 1572868
  36.0 2.0 copy-start.16
  42.0 1.9 copy-start.17
  42.0 8.8 %copy-start.15 = (f32[1,128,2,128]{3,1,2,0:T(8,128)S(1)}, f32[1,128,2,128]{3,1,2,0:T(8,128)}, u32[]{:S(2)}) copy-start(f32[1,128,2,128]{3,1,2,0:T(8,128)} %convolution_bitcast_fusion.5) | copy-start | bytes 393220
  42.0 9.5 %copy-start.2 = (bf16[128,4,4,256]{0,3,2,1:T(8,128)(2,1)S(1)}, bf16[128,4,4,256]{0,3,2,1:T(8,128)(2,1)}, u32[]{:S(2)}) copy-start(bf16[128,4,4,256]{0,3,2,1:T(8,128)(2,1)} %copy.169) | copy-start | bytes 3145732
  43.6 2.1 %copy-start.5 = (bf16[2,8,128,128]{2,3,1,0:T(8,128)(2,1)}, bf16[2,8,128,128]{2,3,1,0:T(8,128)(2,1)S(1)}, u32[]{:S(2)}) copy-start(bf16[2,8,128,128]{2,3,1,0:T(8,128)(2,1)S(1)} %fusion.11) | copy-start | bytes 1572868
  44.0 6.9 %collective-permute-start.1 = (bf16[2,128,2,128]{3,1,2,0:T(8,128)(2,1)S(1)}, bf16[2,128,2,128]{3,1,2,0:T(8,128)(2,1)S(1)}, u32[]{:S(2)}, u32[]{:S(2)}) collective-permute-start(bf16[2,128,2,128]{3,1,2,0:T(8,128)(2,1)S(1)} %pad_maximum_fusion.1), channel_id=1, source_target_pairs={{8,0},{16,8},{24,16},{9,1},{17,9},{25,17},{10,2},{18,10},{26,18},{... | collective-permute-start | bytes 393224 | tf_op jit(solution)/shard_map/ppermute | solution.py:35
  50.9 0.6 copy-start.9
  54.2 1.2 copy-start.7
  54.2 2.5 %copy-start.8 = (f32[1024,256]{1,0:T(8,128)S(1)}, f32[1024,256]{1,0:T(8,128)}, u32[]{:S(2)}) copy-start(f32[1024,256]{1,0:T(8,128)} %param.21) | copy-start | bytes 3145732
  54.2 6.7 %copy-start.6 = (bf16[2,8,128,128]{2,3,1,0:T(8,128)(2,1)S(1)}, bf16[2,8,128,128]{2,3,1,0:T(8,128)(2,1)}, u32[]{:S(2)}) copy-start(bf16[2,8,128,128]{2,3,1,0:T(8,128)(2,1)} %copy-done.5) | copy-start | bytes 1572868
  56.7 3.8 %copy-start.12 = (bf16[128,2,128,1]{2,0,3,1:T(8,128)(2,1)S(1)}, bf16[128,2,128,1]{2,0,3,1:T(8,128)(2,1)}, u32[]{:S(2)}) copy-start(bf16[128,2,128,1]{2,0,3,1:T(8,128)(2,1)} %copy-done.11) | copy-start | bytes 196612
  152.4 8.3 %copy-start.10 = (bf16[1,128,2,128]{3,1,2,0:T(8,128)(2,1)S(1)}, bf16[1,128,2,128]{3,1,2,0:T(8,128)(2,1)}, u32[]{:S(2)}) copy-start(bf16[1,128,2,128]{3,1,2,0:T(8,128)(2,1)} %copy-done.9) | copy-start | bytes 196612
  152.4 6.6 %collective-permute-start.2 = (f32[256,256]{0,1:T(8,128)}, f32[256,256]{0,1:T(8,128)S(1)}, u32[]{:S(2)}, u32[]{:S(2)}) collective-permute-start(f32[256,256]{0,1:T(8,128)} %reduce-scatter.2.cloned.1.call-done), channel_id=1, source_target_pairs={{0,8},{8,0},{16,24},{24,16},{1,9},{9,1},{17,25},{25,17},{2,10},{10... | collective-permute-start | bytes 786440 | tf_op jit(solution)/shard_map/ppermute | solution.py:24
  153.6 32.8 %copy-start = (f32[1024,256]{0,1:T(8,128)S(1)}, f32[1024,256]{0,1:T(8,128)}, u32[]{:S(2)}) copy-start(f32[1024,256]{0,1:T(8,128)} %copy.166) | copy-start | bytes 3145732
  153.6 32.8 %copy-start.1 = (f32[1024,256]{0,1:T(8,128)S(1)}, f32[1024,256]{0,1:T(8,128)}, u32[]{:S(2)}) copy-start(f32[1024,256]{0,1:T(8,128)} %copy.170) | copy-start | bytes 3145732
  160.1 9.9 %collective-permute-start.3 = (f32[512,256]{0,1:T(8,128)S(1)}, f32[512,256]{0,1:T(8,128)S(1)}, u32[]{:S(2)}, u32[]{:S(2)}) collective-permute-start(f32[512,256]{0,1:T(8,128)S(1)} %maximum_select_fusion.1), channel_id=1, source_target_pairs={{0,16},{8,24},{16,0},{24,8},{1,17},{9,25},{17,1},{25,9},{2,18},{10... | collective-permute-start | bytes 1572872 | tf_op jit(solution)/shard_map/ppermute | solution.py:24
  190.0 5.2 %copy-start.3 = (f32[1024,256]{0,1:T(8,128)S(1)}, f32[1024,256]{0,1:T(8,128)}, u32[]{:S(2)}) copy-start(f32[1024,256]{0,1:T(8,128)} %get-tuple-element.37) | copy-start | bytes 3145732
Sparse Core Ops, SparseCore 0:
  54.3 98.0 reduce-scatter.1
